TPU v7x, 32 devices: a whole 2x2x4 slice. The times are simulated.
32 devices in a mesh: groups: 2 (over y), seq: 4 (over z), tensor: 4 (over x, core).
Axes of the slice: x: 2, y: 2, z: 4, core: 2. Of those that a mesh axis runs over, the one named last changes fastest.
Arguments:
- x_in: bfloat16 [4096, 5120], P(('groups', 'seq'), 'tensor'), parts along dimension 0, may hold values from -6 to 6
- z_gate: bfloat16 [4096, 5120], P(('groups', 'seq'), 'tensor'), parts along dimension 0, may hold values from -32 to 32
- bc_in: bfloat16 [4096, 256], P(('groups', 'seq')), parts along dimension 0, may hold values from -6 to 6
- step_size: float32 [80, 4096], P('tensor', ('groups', 'seq')), parts along dimension 1, may hold values from 0 to 0.4
- log_keep: float32 [80, 4096], P('tensor', ('groups', 'seq')), parts along dimension 1, may hold values from -1 to 0
- skip_gain: float32 [80], P('tensor'), may hold values from 0.5 to 2
- conv_x: bfloat16 [4, 5120], P(None, 'tensor'), may hold values from -3 to 3
- conv_bc: bfloat16 [4, 256], replicated, may hold values from -3 to 3
- norm_gain: float32 [5120], P('tensor'), may hold values from 0.1 to 1.9
- seg_ends: int32 [1024], P(('groups', 'seq')), parts along dimension 0, may hold values from 0 to 2047, as said below
- pool_query: bfloat16 [320, 5120], P(('groups', 'seq'), 'tensor'), parts along dimension 0, may hold values from -64 to 64
- pool_start: int32 [320], P(('groups', 'seq')), parts along dimension 0, may hold values from 0 to 255, as said below
- pool_stop: int32 [320], P(('groups', 'seq')), parts along dimension 0, may hold values from 64 to 512
Outputs:
- mixed_seq: bfloat16 [4096, 5120], P(('groups', 'seq'), 'tensor'), parts along dimension 0
- pooled: float32 [320, 5120], P(('groups', 'seq'), 'tensor'), parts along dimension 0
There are 2 independent parts, one for each index of `groups`. A program takes and returns all parts, laid end to end along the dimension named above; an argument that names none is the same for every part. Nothing has to cross between parts.
Inputs may be any that keep to these rules, and one draw needn't show every extreme that they name: The tokens fall into blocks of 512; block b holds exactly the 128 segment ends seg_ends[b * 128] to seg_ends[(b + 1) * 128 - 1], strictly increasing. pool_start < pool_stop for every pooled row.
All inputs are finite; a program needn't handle non-finite values.
Results may differ from a plain program's by a relative error of at most 0.039.
Values may be sent and summed in bfloat16 or wider, within the bound.
No kernel may reach another device: no remote copies, remote signals or barrier semaphores. Data moves between devices by JAX's collectives and lax.ppermute only.
A program may use at most 64 MiB of HBM per device.

v0:
```python
import math
import jax
import jax.numpy as jnp
from jax import lax
from jax.sharding import PartitionSpec as P

STRETCH = 256
POOL_HEADS = 32
EPSILON = 1e-05
MASKED = -1e30


def passed_along(value, axis, steps):
    count = lax.axis_size(axis)
    leading, last = (max(0, -steps), min(count, count - steps))
    return lax.ppermute(value, axis, [(source, source + steps) for source in range(leading, last)])


def prefix(part, axis, combine, identity):
    place = lax.axis_index(axis)
    gathered = jax.tree.map(lambda a: lax.all_gather(a, axis), part)
    state = jax.tree.map(lambda a, e: jnp.zeros_like(a) + jnp.asarray(e, a.dtype), part, identity)

    def one(lap, state):
        return combine(
            state, jax.tree.map(lambda a: lax.dynamic_index_in_dim(a, lap, 0, False), gathered)
        )

    return lax.fori_loop(0, place, one, state)


def silu_act(values):
    return values / (1.0 + jnp.exp(-values))


def causal_conv(before, current, weights):
    kernel_width = weights.shape[0]
    length = current.shape[0]
    padded = jnp.concatenate([before, current], axis=0)
    summed = jnp.zeros(current.shape, jnp.float32)
    for offset in range(kernel_width):
        summed = summed + padded[offset : offset + length].astype(jnp.float32) * weights[
            offset
        ].astype(jnp.float32)
    return silu_act(summed).astype(jnp.bfloat16)


def stretch_local(x_block, b_block, c_block, step_block, keep_block):
    block_len = x_block.shape[0]
    cumul_keep = jnp.cumsum(keep_block, axis=1)
    lower_mask = lax.broadcasted_iota(jnp.int32, (block_len, block_len), 0) >= lax.broadcasted_iota(
        jnp.int32, (block_len, block_len), 1
    )
    inner_prod = jnp.einsum("is,js->ij", c_block, b_block, preferred_element_type=jnp.float32)
    spread = cumul_keep[:, :, None] - cumul_keep[:, None, :]
    decay_mask = jnp.where(lower_mask[None], jnp.exp(jnp.where(lower_mask[None], spread, 0.0)), 0.0)
    mixing = (decay_mask * inner_prod[None] * step_block[:, None, :]).astype(jnp.bfloat16)
    intra_part = jnp.einsum("hij,jhp->ihp", mixing, x_block, preferred_element_type=jnp.float32)
    tail_weight = jnp.exp(cumul_keep[:, -1:] - cumul_keep) * step_block
    weighted = (tail_weight.T[:, :, None] * x_block.astype(jnp.float32)).astype(jnp.bfloat16)
    stretch_state = jnp.einsum("jhp,js->hps", weighted, b_block, preferred_element_type=jnp.float32)
    return (intra_part, stretch_state, cumul_keep)


def combine(earlier, later):
    return (earlier[0] * jnp.exp(later[1])[:, None, None] + later[0], earlier[1] + later[1])


def read_state(c_block, state_in):
    state_high = state_in.astype(jnp.bfloat16)
    state_low = (state_in - state_high.astype(jnp.float32)).astype(jnp.bfloat16)
    high_part = jnp.einsum("is,hps->ihp", c_block, state_high, preferred_element_type=jnp.float32)
    low_part = jnp.einsum("is,hps->ihp", c_block, state_low, preferred_element_type=jnp.float32)
    return high_part + low_part


def local(
    x_in,
    z_gate,
    bc_in,
    step_size,
    log_keep,
    skip_gain,
    conv_x,
    conv_bc,
    norm_gain,
    seg_ends,
    pool_query,
    pool_start,
    pool_stop,
):
    tok_rows = x_in.shape[0]
    channels = x_in.shape[1]
    heads_local = step_size.shape[0]
    head_width = channels // heads_local
    state_width = bc_in.shape[1] // 2
    rim_rows = conv_x.shape[0] - 1
    edge_rows = jnp.concatenate([x_in[tok_rows - rim_rows :], bc_in[tok_rows - rim_rows :]], axis=1)
    before = passed_along(edge_rows, "seq", 1)
    x_conv = causal_conv(before[:, :channels], x_in, conv_x)
    bc_conv = causal_conv(before[:, channels:], bc_in, conv_bc)
    b_mat = bc_conv[:, :state_width]
    c_mat = bc_conv[:, state_width:]
    x_heads = x_conv.reshape(tok_rows, heads_local, head_width)
    stretch_count = tok_rows // STRETCH
    entry_state = jnp.zeros((heads_local, head_width, state_width), jnp.float32)
    decay_total = jnp.zeros((heads_local,), jnp.float32)
    saved_parts = []
    for block_index in range(stretch_count):
        first_row = block_index * STRETCH
        last_row = first_row + STRETCH
        intra_part, stretch_state, cumul_keep = stretch_local(
            x_heads[first_row:last_row],
            b_mat[first_row:last_row],
            c_mat[first_row:last_row],
            step_size[:, first_row:last_row],
            log_keep[:, first_row:last_row],
        )
        saved_parts.append((intra_part, cumul_keep, entry_state, decay_total))
        entry_state = jnp.exp(cumul_keep[:, -1])[:, None, None] * entry_state + stretch_state
        decay_total = decay_total + cumul_keep[:, -1]
    incoming, unused = prefix(
        (entry_state, decay_total),
        "seq",
        combine,
        (jnp.zeros_like(entry_state), jnp.zeros_like(decay_total)),
    )
    pieces_out = []
    for block_index in range(stretch_count):
        intra_part, cumul_keep, entry_part, decay_part = saved_parts[block_index]
        first_row = block_index * STRETCH
        state_in = entry_part + jnp.exp(decay_part)[:, None, None] * incoming
        from_state = read_state(c_mat[first_row : first_row + STRETCH], state_in)
        pieces_out.append(intra_part + jnp.exp(cumul_keep).T[:, :, None] * from_state)
    ssd_out = jnp.concatenate(pieces_out, axis=0) + skip_gain[None, :, None] * x_heads.astype(
        jnp.float32
    )
    gated = ssd_out.reshape(tok_rows, channels) * silu_act(z_gate.astype(jnp.float32))
    square_sum = lax.psum(jnp.sum(gated * gated, axis=1), "tensor")
    width_all = channels * lax.axis_size("tensor")
    mixed_seq = (
        gated * lax.rsqrt(square_sum / width_all + EPSILON)[:, None] * norm_gain[None, :]
    ).astype(jnp.bfloat16)
    local_ends = seg_ends - lax.axis_index("seq") * tok_rows
    summaries = jnp.take(mixed_seq, local_ends, axis=0)
    pool_heads_local = POOL_HEADS // lax.axis_size("tensor")
    pool_width = channels // pool_heads_local
    scale_factor = 1.0 / math.sqrt(pool_width)
    pools_local = pool_query.shape[0]
    queries = pool_query.reshape(pools_local, pool_heads_local, pool_width)
    piece = lax.all_gather(summaries, "seq", axis=0, tiled=True)
    peak = jnp.full((pool_heads_local, pools_local), MASKED, jnp.float32)
    numer = jnp.zeros((pools_local, pool_heads_local, pool_width), jnp.float32)
    count = piece.shape[0]
    seg_index = lax.iota(jnp.int32, count)
    inside = (seg_index[None, :] >= pool_start[:, None]) & (seg_index[None, :] < pool_stop[:, None])
    keys_block = piece.reshape(count, pool_heads_local, pool_width)
    logits = (
        jnp.einsum("pad,rad->apr", queries, keys_block, preferred_element_type=jnp.float32)
        * scale_factor
    )
    logits = jnp.where(inside[None], logits, MASKED)
    new_peak = jnp.maximum(peak, jnp.max(logits, axis=2))
    expo = jnp.where(inside[None], jnp.exp(logits - new_peak[:, :, None]), 0.0)
    rescale = jnp.exp(peak - new_peak)
    denom = jnp.sum(expo, axis=2)
    numer = numer * rescale.T[:, :, None] + jnp.einsum(
        "apr,rad->pad", expo.astype(jnp.bfloat16), keys_block, preferred_element_type=jnp.float32
    )
    peak, denom, numer = (new_peak, denom, numer)
    pooled = (numer / denom.T[:, :, None]).reshape(pools_local, channels)
    return (mixed_seq, pooled)


def solution(mesh):
    in_specs = (
        P(("groups", "seq"), "tensor"),
        P(("groups", "seq"), "tensor"),
        P(("groups", "seq"), None),
        P("tensor", ("groups", "seq")),
        P("tensor", ("groups", "seq")),
        P("tensor"),
        P(None, "tensor"),
        P(),
        P("tensor"),
        P(("groups", "seq")),
        P(("groups", "seq"), "tensor"),
        P(("groups", "seq")),
        P(("groups", "seq")),
    )
    out_specs = (P(("groups", "seq"), "tensor"), P(("groups", "seq"), "tensor"))
    return jax.shard_map(local, mesh=mesh, in_specs=in_specs, out_specs=out_specs, check_vma=False)
```

profile of v0, /device:TPU:0, one launch (start us, length us, event | category | flops | bytes accessed | tf_op | source)
XLA Modules:
  0.0 157.4 jit_solution(5044019205403970520)
XLA Ops:
  7.2 0.7 slice.120
  7.9 0.7 slice.121
  8.7 5.0 %collective-permute-start = (bf16[3,1536]{1,0:T(4,128)(2,1)S(1)}, bf16[3,1536]{1,0:T(4,128)(2,1)S(1)}, u32[]{:S(2)}, u32[]{:S(2)}) collective-permute-start(bf16[3,1536]{1,0:T(4,128)(2,1)S(1)} %pad_maximum_fusion.2), channel_id=1, source_target_pairs={{0,4},{4,8},{8,12},{1,5},{5,9},{9,13},{2,6},{6,10},{10,14},{3,7},{... | collective-permute-start | bytes 27656 | tf_op jit(solution)/shard_map/ppermute | solution.py:16
  13.6 0.8 fusion.71
  14.4 0.6 reduce-window.14
  15.4 0.6 reduce-window.16
  16.3 0.8 slice_convert_fusion.3
  17.2 0.8 slice_reduce_fusion.2
  17.9 0.5 fusion.72
  18.5 1.5 fusion.70
  19.9 0.9 convert_reduce_fusion.3
  20.8 0.6 exp.65
  21.5 4.0 %divide_convert_fusion = bf16[512,1280]{1,0:T(8,128)(2,1)S(1)} fusion(bf16[512,1280]{1,0:T(8,128)(2,1)} %param.15, bf16[3,1280]{1,0:T(4,128)(2,1)S(1)} %slice.158, f32[1280]{0:T(1024)S(1)} %get-tuple-element.52, f32[1280]{0:T(1024)S(1)} %get-tuple-element.53, f32[1280]{0:T(1024)S(1)} %get-tuple-element.51, f32[1280]{0:T(1024)S(1)} %get-tuple-element.50), kind=kLoop, calls=%fused_computation.25 | loop fusion | flops 15728640 | bytes 2649600 | tf_op jit(solution)/shard_map/convert_element_type | solution.py:45
  25.6 0.2 copy.34
  25.8 0.2 copy.39
  26.1 1.9 %divide_convert_fusion.1 = bf16[512,256]{1,0:T(8,128)(2,1)S(1)} fusion(bf16[512,256]{1,0:T(8,128)(2,1)} %param.17, bf16[3,256]{1,0:T(4,128)(2,1)S(1)} %slice.165, f32[256]{0:T(256)S(1)} %bitcast.90, f32[256]{0:T(256)S(1)} %bitcast.91, f32[256]{0:T(256)S(1)} %bitcast.89, f32[256]{0:T(256)S(1)} %bitcast.88), kind=kLoop, calls=%fused_computation.59 | loop fusion | flops 3145728 | bytes 529920 | tf_op jit(solution)/shard_map/convert_element_type | solution.py:45
  28.0 1.1 convolution_add_fusion.3
  29.1 1.9 %convolution_add_fusion.2 = f32[20,64,128]{2,1,0:T(8,128)} fusion(bf16[256,20,64]{0,2,1:T(8,128)(2,1)S(1)} %bitcast.75, f32[256,20]{0,1:T(8,128)} %get-tuple-element.72, f32[20,64,128]{2,1,0:T(8,128)S(1)} %convolution_add_fusion.3, f32[20]{0:T(128)} %exp.65, bf16[512,256]{1,0:T(8,128)(2,1)S(1)} %divide_convert_fusion.1), kind=kOutput, calls=%fused_computation.43 | convolution fusion | flops 85196800 | bytes 2052176 | tf_op jit(solution)/shard_map/jhp,js->hps/dot_general | solution.py:61
  31.1 1.2 dynamic-slice
  33.0 0.9 dynamic-update-slice
  33.8 10.1 %all-reduce = f32[80]{0:T(128)S(1)} all-reduce(f32[80]{0:T(128)S(1)} %dynamic-update-slice), channel_id=2, replica_groups=mesh['groups'=2,'seq'=4,'tensor'=4] {'seq'}, use_global_device_ids=true, to_apply=%add | all-reduce | flops 80 | bytes 640
  44.1 0.7 mul.319
  44.8 0.7 mul.320
  45.4 0.7 compare_and_fusion
  46.5 3.7 %fusion.18 = f32[256,20,64]{0,2,1:T(8,128)} fusion(bf16[256,20,64]{0,2,1:T(8,128)(2,1)S(1)} %bitcast.78, f32[20,256]{1,0:T(8,128)} %get-tuple-element.70, f32[256,256]{1,0:T(8,128)S(1)} %fusion.57, f32[20,256]{1,0:T(8,128)} %bitcast.81, pred[256,256]{1,0:T(8,128)(4,1)S(1)} %iota_compare_fusion), kind=kOutput, calls=%fused_computation.31 | convolution fusion | flops 175636480 | bytes 2334720 | tf_op jit(solution)/shard_map/hij,jhp->ihp/dot_general | solution.py:58
  50.3 2.9 %fusion.17 = f32[256,20,64]{0,2,1:T(8,128)} fusion(bf16[256,20,64]{0,2,1:T(8,128)(2,1)S(1)} %bitcast.76, f32[20,256]{1,0:T(8,128)S(1)} %copy-done.11, f32[256,256]{1,0:T(8,128)S(1)} %fusion.53, f32[20,256]{1,0:T(8,128)S(1)} %bitcast.84, pred[256,256]{1,0:T(8,128)(4,1)S(1)} %iota_compare_fusion), kind=kOutput, calls=%fused_computation.30 | convolution fusion | flops 175636480 | bytes 2334720 | tf_op jit(solution)/shard_map/hij,jhp->ihp/dot_general | solution.py:58
  53.1 33.0 %all-gather.7.cloned.1.call-done = f32[80,64,128]{2,1,0:T(8,128)} async-done(((f32[20,64,128]{2,1,0:T(8,128)}), f32[80,64,128]{2,1,0:T(8,128)}) %all-gather.7.cloned.1.call-update) | async-done | bytes 2621456 | tf_op jit(solution)/shard_map/all_gather | solution.py:21
  86.3 0.3 fusion.44
  86.6 0.4 copy-done.9
  87.0 0.6 copy-done.3
  87.6 1.4 fusion.21
  89.0 2.8 %copy.40 = f32[256,1280]{1,0:T(8,128)} copy(f32[256,1280]{0,1:T(8,128)} %bitcast.73) | data formatting | bytes 2621440 | tf_op jit(solution)/shard_map/concatenate | solution.py:135
  91.8 0.4 fusion.41
  92.2 0.9 copy-done.2
  93.1 1.4 fusion.22
  94.6 2.9 %copy.41 = f32[256,1280]{1,0:T(8,128)} copy(f32[256,1280]{0,1:T(8,128)} %bitcast.72) | data formatting | bytes 2621440 | tf_op jit(solution)/shard_map/concatenate | solution.py:135
  97.5 4.2 %multiply_reduce_fusion = (f32[512]{0:T(512)S(1)}, f32[512,1280]{1,0:T(8,128)}) fusion(bf16[512,1280]{1,0:T(8,128)(2,1)} %param.16, bf16[512,1280]{1,0:T(8,128)(2,1)S(1)} %divide_convert_fusion, f32[1280]{0:T(1024)S(1)} %copy-done.10, f32[256,1280]{1,0:T(8,128)} %copy.41, f32[256,1280]{1,0:T(8,128)S(1)} %copy-done.1), kind=kLoop, calls=%fused_computation.14 | loop fusion | flops 7208448 | bytes 7871488 | tf_op jit(solution)/shard_map/reduce_sum | solution.py:139
  101.7 6.4 %psum.7 = f32[512]{0:T(512)S(1)} all-reduce(f32[512]{0:T(512)S(1)} %get-tuple-element.66), channel_id=1, replica_groups=mesh['groups'=2,'seq'=4,'tensor'=4] {'tensor'}, use_global_device_ids=true, to_apply=%region_7.8 | all-reduce | flops 512 | bytes 4096 | tf_op jit(solution)/shard_map/psum | solution.py:139
  108.1 2.0 %multiply_convert_fusion.4 = bf16[512,1280]{1,0:T(8,128)(2,1)S(1)} fusion(f32[512,1280]{1,0:T(8,128)} %get-tuple-element.67, f32[1280]{0:T(1024)S(1)} %copy-done.12, f32[512]{0:T(512)S(1)} %add_rsqrt_fusion), kind=kLoop, calls=%fused_computation.13 | loop fusion | flops 1966080 | bytes 3939328 | tf_op jit(solution)/shard_map/convert_element_type | solution.py:143
  110.2 0.9 gather_fusion
  111.1 0.8 broadcast_select_fusion
  112.0 0.2 reshape.192
  112.3 34.4 %all-gather.5.cloned.1.call-done = bf16[512,1280]{1,0:T(8,128)(2,1)} async-done(((bf16[128,1280]{1,0:T(8,128)(2,1)}), bf16[512,1280]{1,0:T(8,128)(2,1)}) %all-gather.5.cloned.1.call-update) | async-done | bytes 1310736 | tf_op jit(solution)/shard_map/all_gather | solution.py:151
  146.7 1.6 %copy.42 = bf16[512,1280]{0,1:T(8,128)(2,1)S(1)} copy(bf16[512,1280]{1,0:T(8,128)(2,1)} %all-gather.5.cloned.1.call-done) | data formatting | bytes 2621440 | tf_op jit(solution)/shard_map/all_gather | solution.py:151
  148.3 0.4 fusion.73
  148.7 0.3 fusion.31
  149.0 0.6 fusion.28
  149.7 0.8 reshape.193
  (68 shorter events, 1.7 us)
Async XLA Ops:
  7.2 79.0 %all-gather.7.cloned.1.call-start = ((), (), s32[]{:S(2)}) async-start(), calls=%async_computation.1 | async-start | bytes 3276800 | tf_op jit(solution)/shard_map/all_gather | solution.py:21
  8.7 12.8 %collective-permute-start = (bf16[3,1536]{1,0:T(4,128)(2,1)S(1)}, bf16[3,1536]{1,0:T(4,128)(2,1)S(1)}, u32[]{:S(2)}, u32[]{:S(2)}) collective-permute-start(bf16[3,1536]{1,0:T(4,128)(2,1)S(1)} %pad_maximum_fusion.2), channel_id=1, source_target_pairs={{0,4},{4,8},{8,12},{1,5},{5,9},{9,13},{2,6},{6,10},{10,14},{3,7},{... | collective-permute-start | bytes 27656 | tf_op jit(solution)/shard_map/ppermute | solution.py:16
  15.3 6.1 %copy-start.4 = (f32[3,8,2,128]{3,1,2,0:T(8,128)}, f32[3,8,2,128]{3,1,2,0:T(8,128)S(1)}, u32[]{:S(2)}) copy-start(f32[3,8,2,128]{3,1,2,0:T(8,128)S(1)} %copy.45) | copy-start | bytes 73732
  16.3 5.1 %copy-start.5 = (f32[3,8,2,128]{3,1,2,0:T(8,128)}, f32[3,8,2,128]{3,1,2,0:T(8,128)S(1)}, u32[]{:S(2)}) copy-start(f32[3,8,2,128]{3,1,2,0:T(8,128)S(1)} %copy.46) | copy-start | bytes 73732
  31.0 115.7 %all-gather.5.cloned.1.call-start = ((), (), s32[]{:S(2)}) async-start(), calls=%async_computation | async-start | bytes 1638400 | tf_op jit(solution)/shard_map/all_gather | solution.py:151
  46.5 3.7 %copy-start.6 = (f32[3,8,2,128]{3,1,2,0:T(8,128)S(1)}, f32[3,8,2,128]{3,1,2,0:T(8,128)}, u32[]{:S(2)}) copy-start(f32[3,8,2,128]{3,1,2,0:T(8,128)} %copy-done.5) | copy-start | bytes 73732
  46.5 3.7 %copy-start.11 = (f32[20,256]{1,0:T(8,128)S(1)}, f32[20,256]{1,0:T(8,128)}, u32[]{:S(2)}) copy-start(f32[20,256]{1,0:T(8,128)} %get-tuple-element.73) | copy-start | bytes 61444
  86.3 0.7 copy-start.9
  86.3 1.3 copy-start.3
  87.6 4.2 %copy-start.13 = (f32[20]{0:T(128)S(1)}, f32[20]{0:T(128)}, u32[]{:S(2)}) copy-start(f32[20]{0:T(128)} %get-tuple-element.84) | copy-start | bytes 244
  89.0 3.2 %copy-start.8 = (f32[256,20]{0,1:T(8,128)S(1)}, f32[256,20]{0,1:T(8,128)}, u32[]{:S(2)}) copy-start(f32[256,20]{0,1:T(8,128)} %get-tuple-element.76) | copy-start | bytes 61444
  91.8 1.3 copy-start.2
  94.6 2.9 %copy-start.1 = (f32[256,1280]{1,0:T(8,128)S(1)}, f32[256,1280]{1,0:T(8,128)}, u32[]{:S(2)}) copy-start(f32[256,1280]{1,0:T(8,128)} %copy.40) | copy-start | bytes 3932164
  94.6 2.9 %copy-start.10 = (f32[1280]{0:T(1024)S(1)}, f32[1280]{0:T(1024)}, u32[]{:S(2)}) copy-start(f32[1280]{0:T(1024)} %mul.320) | copy-start | bytes 15364
  97.5 10.6 %copy-start.12 = (f32[1280]{0:T(1024)S(1)}, f32[1280]{0:T(1024)}, u32[]{:S(2)}) copy-start(f32[1280]{0:T(1024)} %param.23) | copy-start | bytes 15364
  110.1 38.2 %copy-start = (bf16[512,1280]{1,0:T(8,128)(2,1)}, bf16[512,1280]{1,0:T(8,128)(2,1)S(1)}, u32[]{:S(2)}) copy-start(bf16[512,1280]{1,0:T(8,128)(2,1)S(1)} %multiply_convert_fusion.4) | copy-start | bytes 3932164
  110.2 1.8 %copy-start.7 = (bf16[40,1280]{1,0:T(8,128)(2,1)S(1)}, bf16[40,1280]{1,0:T(8,128)(2,1)}, u32[]{:S(2)}) copy-start(bf16[40,1280]{1,0:T(8,128)(2,1)} %param.25) | copy-start | bytes 307204
  110.2 2.0 %copy-start.14 = (s32[40]{0:T(128)S(1)}, s32[40]{0:T(128)}, u32[]{:S(2)}) copy-start(s32[40]{0:T(128)} %param.27) | copy-start | bytes 484
  110.2 2.0 %copy-start.15 = (s32[40]{0:T(128)S(1)}, s32[40]{0:T(128)}, u32[]{:S(2)}) copy-start(s32[40]{0:T(128)} %param.26) | copy-start | bytes 484
Sparse Core Ops, SparseCore 0:
  31.1 55.0 all-gather.6
  112.1 34.5 all-gather.4
where the time goes:
time: 158 us; the launch traced here: 157 us
  waiting for transfers between devices  67.5 us (43%)
  other arithmetic  20 us (13%)
  local copies, waits for them, and re-layouts  18.7 us (12%)
  blocking collectives  16.5 us (10%)
  between operations  15.1 us (10%)
  matrix products  14.5 us (9%)
  starting transfers between devices  5.04 us (3%)
    all_gather x1, waiting for transfers between devices, local(): piece = lax.all_gather(summaries, 'seq', axis=0, tiled=True)  34.4 us
    all_gather x1, waiting for transfers between devices, prefix(): gathered = jax.tree.map(lambda a: lax.all_gather(a, axis), part)  33 us
    unnamed x1, blocking collectives  10.1 us
    dot_general x2, matrix products, stretch_local(): jnp.einsum('hij,jhp->ihp', mixing, x_block, preferred_element_type=jnp.fl...  6.59 us
    psum x1, blocking collectives, local(): square_sum = lax.psum(jnp.sum(gated * gated, axis=1), 'tensor')  6.37 us
    convert_element_type x2, other arithmetic, causal_conv(): return silu_act(summed).astype(jnp.bfloat16)  5.91 us
    concatenate x2, local copies, waits for them, and re-layouts, local(): jnp.concatenate(pieces_out, axis=0)  5.7 us
    ppermute x1, starting transfers between devices, passed_along(): lax.ppermute(value, axis, [(source, source + steps) for source in range(l...  4.96 us
  transfers between devices with their start and end apart: 3, of which 2 were waited for; matrix products, arithmetic and copies ran while one was open for 12% of the time, Pallas kernels for 0%

commit v1 on v0

--- a/solution.py
+++ b/solution.py
@@ -148,7 +148,14 @@
     scale_factor = 1.0 / math.sqrt(pool_width)
     pools_local = pool_query.shape[0]
     queries = pool_query.reshape(pools_local, pool_heads_local, pool_width)
-    piece = lax.all_gather(summaries, "seq", axis=0, tiled=True)
+    ways, here, step = (lax.axis_size("seq"), lax.axis_index("seq"), summaries.shape[0])
+    line, have = (summaries, 1)
+    while have < ways:
+        line = jnp.concatenate(
+            [line, lax.ppermute(line, "seq", [(d, (d - have) % ways) for d in range(ways)])], axis=0
+        )
+        have = 2 * have
+    piece = jnp.roll(line, here * step, axis=0)
     peak = jnp.full((pool_heads_local, pools_local), MASKED, jnp.float32)
     numer = jnp.zeros((pools_local, pool_heads_local, pool_width), jnp.float32)
     count = piece.shape[0]

time: 158 us -> 168 us (1.063)
  starting transfers between devices: 5.04 us -> 11.6 us
  local copies, waits for them, and re-layouts: 18.7 us -> 23.2 us
  waiting for transfers between devices: 67.5 us -> 65.2 us
    all_gather x1 -> x0, waiting for transfers between devices: 34.4 us -> none  [local(): piece = lax.all_gather(summaries, 'seq', axis=0, tiled=True)]
    ppermute x0 -> x2, waiting for transfers between devices: none -> 32.1 us  [local(): lax.ppermute(line, 'seq', [(d, (d - have) % ways) for d in range(ways)])]
    ppermute x0 -> x2, starting transfers between devices: none -> 6.57 us  [local(): lax.ppermute(line, 'seq', [(d, (d - have) % ways) for d in range(ways)])]
    unnamed x39 -> x41, local copies, waits for them, and re-layouts: 4.11 us -> 7.25 us
    dynamic_slice x0 -> x2, local copies, waits for them, and re-layouts: none -> 2.05 us  [local(): piece = jnp.roll(line, here * step, axis=0)]
  transfers between devices with their start and end apart: 3 -> 4, of which waited for: 2 -> 3; matrix products, arithmetic and copies ran while one was open for 12% -> 12% of each run, Pallas kernels for 0% -> 0%
where the time goes in v1:
time: 168 us; the launch traced here: 167 us
  waiting for transfers between devices  65.2 us (39%)
  local copies, waits for them, and re-layouts  23.2 us (14%)
  other arithmetic  20.7 us (12%)
  blocking collectives  16.5 us (10%)
  between operations  15.1 us (9%)
  matrix products  14.5 us (9%)
  starting transfers between devices  11.6 us (7%)
    all_gather x1, waiting for transfers between devices, prefix(): gathered = jax.tree.map(lambda a: lax.all_gather(a, axis), part)  33.1 us
    ppermute x2, waiting for transfers between devices, local(): lax.ppermute(line, 'seq', [(d, (d - have) % ways) for d in range(ways)])  32.1 us
    unnamed x1, blocking collectives  10.1 us
    unnamed x41, local copies, waits for them, and re-layouts  7.25 us
    dot_general x2, matrix products, stretch_local(): jnp.einsum('hij,jhp->ihp', mixing, x_block, preferred_element_type=jnp.fl...  6.59 us
    ppermute x2, starting transfers between devices, local(): lax.ppermute(line, 'seq', [(d, (d - have) % ways) for d in range(ways)])  6.57 us
    psum x1, blocking collectives, local(): square_sum = lax.psum(jnp.sum(gated * gated, axis=1), 'tensor')  6.37 us
    convert_element_type x2, other arithmetic, causal_conv(): return silu_act(summed).astype(jnp.bfloat16)  5.91 us
  transfers between devices with their start and end apart: 4, of which 3 were waited for; matrix products, arithmetic and copies ran while one was open for 12% of the time, Pallas kernels for 0%

profile of v1, /device:TPU:0, one launch (start us, length us, event | category | flops | bytes accessed | tf_op | source)
XLA Modules:
  0.0 166.8 jit_solution(15728839836271906276)
XLA Ops:
  7.2 0.7 slice.120
  7.9 0.7 slice.121
  8.7 5.0 %collective-permute-start = (bf16[3,1536]{1,0:T(4,128)(2,1)S(1)}, bf16[3,1536]{1,0:T(4,128)(2,1)S(1)}, u32[]{:S(2)}, u32[]{:S(2)}) collective-permute-start(bf16[3,1536]{1,0:T(4,128)(2,1)S(1)} %pad_maximum_fusion.3), channel_id=1, source_target_pairs={{0,4},{4,8},{8,12},{1,5},{5,9},{9,13},{2,6},{6,10},{10,14},{3,7},{... | collective-permute-start | bytes 27656 | tf_op jit(solution)/shard_map/ppermute | solution.py:16
  13.6 0.8 fusion.71
  14.4 0.6 reduce-window.14
  15.4 0.6 reduce-window.16
  16.3 0.8 slice_convert_fusion.3
  17.2 0.8 slice_reduce_fusion.2
  18.5 1.5 fusion.70
  19.9 0.9 convert_reduce_fusion.3
  20.8 0.6 exp.65
  21.5 4.0 %divide_convert_fusion = bf16[512,1280]{1,0:T(8,128)(2,1)S(1)} fusion(bf16[512,1280]{1,0:T(8,128)(2,1)} %param.15, bf16[3,1280]{1,0:T(4,128)(2,1)S(1)} %slice.158, f32[1280]{0:T(1024)S(1)} %get-tuple-element.52, f32[1280]{0:T(1024)S(1)} %get-tuple-element.53, f32[1280]{0:T(1024)S(1)} %get-tuple-element.51, f32[1280]{0:T(1024)S(1)} %get-tuple-element.50), kind=kLoop, calls=%fused_computation.25 | loop fusion | flops 15728640 | bytes 2649600 | tf_op jit(solution)/shard_map/convert_element_type | solution.py:45
  26.1 1.9 %divide_convert_fusion.1 = bf16[512,256]{1,0:T(8,128)(2,1)S(1)} fusion(bf16[512,256]{1,0:T(8,128)(2,1)} %param.17, bf16[3,256]{1,0:T(4,128)(2,1)S(1)} %slice.165, f32[256]{0:T(256)S(1)} %bitcast.90, f32[256]{0:T(256)S(1)} %bitcast.91, f32[256]{0:T(256)S(1)} %bitcast.89, f32[256]{0:T(256)S(1)} %bitcast.88), kind=kLoop, calls=%fused_computation.60 | loop fusion | flops 3145728 | bytes 529920 | tf_op jit(solution)/shard_map/convert_element_type | solution.py:45
  28.0 1.1 convolution_add_fusion.3
  29.1 1.9 %convolution_add_fusion.2 = f32[20,64,128]{2,1,0:T(8,128)} fusion(bf16[256,20,64]{0,2,1:T(8,128)(2,1)S(1)} %bitcast.75, f32[256,20]{0,1:T(8,128)} %get-tuple-element.74, f32[20,64,128]{2,1,0:T(8,128)S(1)} %convolution_add_fusion.3, f32[20]{0:T(128)} %exp.65, bf16[512,256]{1,0:T(8,128)(2,1)S(1)} %divide_convert_fusion.1), kind=kOutput, calls=%fused_computation.43 | convolution fusion | flops 85196800 | bytes 2052176 | tf_op jit(solution)/shard_map/jhp,js->hps/dot_general | solution.py:61
  31.0 1.2 dynamic-slice
  32.9 0.9 dynamic-update-slice
  33.8 10.1 %all-reduce = f32[80]{0:T(128)S(1)} all-reduce(f32[80]{0:T(128)S(1)} %dynamic-update-slice), channel_id=2, replica_groups=mesh['groups'=2,'seq'=4,'tensor'=4] {'seq'}, use_global_device_ids=true, to_apply=%add | all-reduce | flops 80 | bytes 640
  44.0 0.7 mul.322
  44.7 0.7 mul.323
  45.4 0.7 compare_and_fusion
  46.5 3.7 %fusion.18 = f32[256,20,64]{0,2,1:T(8,128)} fusion(bf16[256,20,64]{0,2,1:T(8,128)(2,1)S(1)} %bitcast.78, f32[20,256]{1,0:T(8,128)} %get-tuple-element.72, f32[256,256]{1,0:T(8,128)S(1)} %fusion.57, f32[20,256]{1,0:T(8,128)} %bitcast.81, pred[256,256]{1,0:T(8,128)(4,1)S(1)} %iota_compare_fusion), kind=kOutput, calls=%fused_computation.31 | convolution fusion | flops 175636480 | bytes 2334720 | tf_op jit(solution)/shard_map/hij,jhp->ihp/dot_general | solution.py:58
  50.2 2.9 %fusion.17 = f32[256,20,64]{0,2,1:T(8,128)} fusion(bf16[256,20,64]{0,2,1:T(8,128)(2,1)S(1)} %bitcast.76, f32[20,256]{1,0:T(8,128)S(1)} %copy-done.11, f32[256,256]{1,0:T(8,128)S(1)} %fusion.53, f32[20,256]{1,0:T(8,128)S(1)} %bitcast.84, pred[256,256]{1,0:T(8,128)(4,1)S(1)} %iota_compare_fusion), kind=kOutput, calls=%fused_computation.30 | convolution fusion | flops 175636480 | bytes 2334720 | tf_op jit(solution)/shard_map/hij,jhp->ihp/dot_general | solution.py:58
  53.1 33.1 %all-gather.4.cloned.1.call-done = f32[80,64,128]{2,1,0:T(8,128)} async-done(((f32[20,64,128]{2,1,0:T(8,128)}), f32[80,64,128]{2,1,0:T(8,128)}) %all-gather.4.cloned.1.call-update) | async-done | bytes 2621456 | tf_op jit(solution)/shard_map/all_gather | solution.py:21
  87.0 0.6 copy-done.3
  87.6 1.4 fusion.21
  89.0 2.8 %copy.40 = f32[256,1280]{1,0:T(8,128)} copy(f32[256,1280]{0,1:T(8,128)} %bitcast.73) | data formatting | bytes 2621440 | tf_op jit(solution)/shard_map/concatenate | solution.py:135
  92.2 0.9 copy-done.2
  93.1 1.4 fusion.22
  94.6 2.9 %copy.41 = f32[256,1280]{1,0:T(8,128)} copy(f32[256,1280]{0,1:T(8,128)} %bitcast.72) | data formatting | bytes 2621440 | tf_op jit(solution)/shard_map/concatenate | solution.py:135
  97.5 4.2 %multiply_reduce_fusion = (f32[512]{0:T(512)S(1)}, f32[512,1280]{1,0:T(8,128)}) fusion(bf16[512,1280]{1,0:T(8,128)(2,1)} %param.16, bf16[512,1280]{1,0:T(8,128)(2,1)S(1)} %divide_convert_fusion, f32[1280]{0:T(1024)S(1)} %copy-done.10, f32[256,1280]{1,0:T(8,128)} %copy.41, f32[256,1280]{1,0:T(8,128)S(1)} %copy-done.1), kind=kLoop, calls=%fused_computation.14 | loop fusion | flops 7208448 | bytes 7871488 | tf_op jit(solution)/shard_map/reduce_sum | solution.py:139
  101.7 6.4 %psum.7 = f32[512]{0:T(512)S(1)} all-reduce(f32[512]{0:T(512)S(1)} %get-tuple-element.68), channel_id=1, replica_groups=mesh['groups'=2,'seq'=4,'tensor'=4] {'tensor'}, use_global_device_ids=true, to_apply=%region_7.8 | all-reduce | flops 512 | bytes 4096 | tf_op jit(solution)/shard_map/psum | solution.py:139
  108.1 2.0 %multiply_convert_fusion.4 = bf16[512,1280]{1,0:T(8,128)(2,1)S(1)} fusion(f32[512,1280]{1,0:T(8,128)} %get-tuple-element.69, f32[1280]{0:T(1024)S(1)} %copy-done.12, f32[512]{0:T(512)S(1)} %add_rsqrt_fusion), kind=kLoop, calls=%fused_computation.13 | loop fusion | flops 1966080 | bytes 3939328 | tf_op jit(solution)/shard_map/convert_element_type | solution.py:143
  110.2 0.9 gather_fusion
  111.1 0.8 constant_dynamic-update-slice_fusion.5
  111.9 5.3 %collective-permute-start.1 = (bf16[128,1280]{1,0:T(8,128)(2,1)S(1)}, bf16[128,1280]{1,0:T(8,128)(2,1)S(1)}, u32[]{:S(2)}, u32[]{:S(2)}) collective-permute-start(bf16[128,1280]{1,0:T(8,128)(2,1)S(1)} %get-tuple-element.65), channel_id=1, source_target_pairs={{0,12},{4,0},{8,4},{12,8},{1,13},{5,1},{9,5},{13,9},{2,14},{6,2},{... | collective-permute-start | bytes 983048 | tf_op jit(solution)/shard_map/ppermute | solution.py:155
  117.2 5.9 %collective-permute-done.1 = bf16[128,1280]{1,0:T(8,128)(2,1)S(1)} collective-permute-done((bf16[128,1280]{1,0:T(8,128)(2,1)S(1)}, bf16[128,1280]{1,0:T(8,128)(2,1)S(1)}, u32[]{:S(2)}, u32[]{:S(2)}) %collective-permute-start.1) | collective-permute-done | bytes 327712 | tf_op jit(solution)/shard_map/ppermute | solution.py:155
  123.2 1.2 collective-permute-start.2
  124.7 0.7 fusion.46
  125.5 0.7 constant_dynamic-update-slice_fusion.4
  126.2 26.1 %collective-permute-done.2 = bf16[256,1280]{1,0:T(8,128)(2,1)S(1)} collective-permute-done((bf16[256,1280]{1,0:T(8,128)(2,1)S(1)}, bf16[256,1280]{1,0:T(8,128)(2,1)S(1)}, u32[]{:S(2)}, u32[]{:S(2)}) %collective-permute-start.2) | collective-permute-done | bytes 655392 | tf_op jit(solution)/shard_map/ppermute | solution.py:155
  152.3 0.9 constant_dynamic-update-slice_fusion.3
  153.2 0.8 constant_dynamic-update-slice_fusion.2
  154.0 0.7 constant_dynamic-update-slice_fusion.1
  154.7 0.9 constant_dynamic-update-slice_fusion
  155.6 1.4 constant_dynamic-slice_fusion
  157.0 0.7 copy.42
  159.1 0.8 reshape.193
  (74 shorter events, 5.2 us)
Async XLA Ops:
  7.2 79.0 %all-gather.4.cloned.1.call-start = ((), (), s32[]{:S(2)}) async-start(), calls=%async_computation | async-start | bytes 3276800 | tf_op jit(solution)/shard_map/all_gather | solution.py:21
  8.7 12.8 %collective-permute-start = (bf16[3,1536]{1,0:T(4,128)(2,1)S(1)}, bf16[3,1536]{1,0:T(4,128)(2,1)S(1)}, u32[]{:S(2)}, u32[]{:S(2)}) collective-permute-start(bf16[3,1536]{1,0:T(4,128)(2,1)S(1)} %pad_maximum_fusion.3), channel_id=1, source_target_pairs={{0,4},{4,8},{8,12},{1,5},{5,9},{9,13},{2,6},{6,10},{10,14},{3,7},{... | collective-permute-start | bytes 27656 | tf_op jit(solution)/shard_map/ppermute | solution.py:16
  15.3 6.1 %copy-start.4 = (f32[3,8,2,128]{3,1,2,0:T(8,128)}, f32[3,8,2,128]{3,1,2,0:T(8,128)S(1)}, u32[]{:S(2)}) copy-start(f32[3,8,2,128]{3,1,2,0:T(8,128)S(1)} %copy.45) | copy-start | bytes 73732
  16.3 5.1 %copy-start.5 = (f32[3,8,2,128]{3,1,2,0:T(8,128)}, f32[3,8,2,128]{3,1,2,0:T(8,128)S(1)}, u32[]{:S(2)}) copy-start(f32[3,8,2,128]{3,1,2,0:T(8,128)S(1)} %copy.46) | copy-start | bytes 73732
  46.5 3.7 %copy-start.6 = (f32[3,8,2,128]{3,1,2,0:T(8,128)S(1)}, f32[3,8,2,128]{3,1,2,0:T(8,128)}, u32[]{:S(2)}) copy-start(f32[3,8,2,128]{3,1,2,0:T(8,128)} %copy-done.5) | copy-start | bytes 73732
  46.5 3.7 %copy-start.11 = (f32[20,256]{1,0:T(8,128)S(1)}, f32[20,256]{1,0:T(8,128)}, u32[]{:S(2)}) copy-start(f32[20,256]{1,0:T(8,128)} %get-tuple-element.75) | copy-start | bytes 61444
  86.3 0.7 copy-start.9
  86.3 1.3 copy-start.3
  87.6 4.2 %copy-start.13 = (f32[20]{0:T(128)S(1)}, f32[20]{0:T(128)}, u32[]{:S(2)}) copy-start(f32[20]{0:T(128)} %get-tuple-element.86) | copy-start | bytes 244
  89.0 3.2 %copy-start.8 = (f32[256,20]{0,1:T(8,128)S(1)}, f32[256,20]{0,1:T(8,128)}, u32[]{:S(2)}) copy-start(f32[256,20]{0,1:T(8,128)} %get-tuple-element.78) | copy-start | bytes 61444
  91.8 1.3 copy-start.2
  94.6 2.9 %copy-start.1 = (f32[256,1280]{1,0:T(8,128)S(1)}, f32[256,1280]{1,0:T(8,128)}, u32[]{:S(2)}) copy-start(f32[256,1280]{1,0:T(8,128)} %copy.40) | copy-start | bytes 3932164
  94.6 2.9 %copy-start.10 = (f32[1280]{0:T(1024)S(1)}, f32[1280]{0:T(1024)}, u32[]{:S(2)}) copy-start(f32[1280]{0:T(1024)} %mul.323) | copy-start | bytes 15364
  97.5 10.6 %copy-start.12 = (f32[1280]{0:T(1024)S(1)}, f32[1280]{0:T(1024)}, u32[]{:S(2)}) copy-start(f32[1280]{0:T(1024)} %param.23) | copy-start | bytes 15364
  110.1 13.1 %copy-start = (bf16[512,1280]{1,0:T(8,128)(2,1)}, bf16[512,1280]{1,0:T(8,128)(2,1)S(1)}, u32[]{:S(2)}) copy-start(bf16[512,1280]{1,0:T(8,128)(2,1)S(1)} %multiply_convert_fusion.4) | copy-start | bytes 3932164
  110.2 14.3 %copy-start.7 = (bf16[40,1280]{1,0:T(8,128)(2,1)S(1)}, bf16[40,1280]{1,0:T(8,128)(2,1)}, u32[]{:S(2)}) copy-start(bf16[40,1280]{1,0:T(8,128)(2,1)} %param.25) | copy-start | bytes 307204
  110.2 14.5 %copy-start.14 = (s32[40]{0:T(128)S(1)}, s32[40]{0:T(128)}, u32[]{:S(2)}) copy-start(s32[40]{0:T(128)} %param.27) | copy-start | bytes 484
  111.9 11.3 %collective-permute-start.1 = (bf16[128,1280]{1,0:T(8,128)(2,1)S(1)}, bf16[128,1280]{1,0:T(8,128)(2,1)S(1)}, u32[]{:S(2)}, u32[]{:S(2)}) collective-permute-start(bf16[128,1280]{1,0:T(8,128)(2,1)S(1)} %get-tuple-element.65), channel_id=1, source_target_pairs={{0,12},{4,0},{8,4},{12,8},{1,13},{5,1},{9,5},{13,9},{2,14},{6,2},{... | collective-permute-start | bytes 983048 | tf_op jit(solution)/shard_map/ppermute | solution.py:155
  123.2 29.1 %collective-permute-start.2 = (bf16[256,1280]{1,0:T(8,128)(2,1)S(1)}, bf16[256,1280]{1,0:T(8,128)(2,1)S(1)}, u32[]{:S(2)}, u32[]{:S(2)}) collective-permute-start(bf16[256,1280]{1,0:T(8,128)(2,1)S(1)} %pad_maximum_fusion.1), channel_id=1, source_target_pairs={{0,8},{4,12},{8,0},{12,4},{1,9},{5,13},{9,1},{13,5},{2,10},{6,14},... | collective-permute-start | bytes 1966088 | tf_op jit(solution)/shard_map/ppermute | solution.py:155
Sparse Core Ops, SparseCore 0:
  31.1 55.0 all-gather.3
